TPU v7x, 32 devices: a whole 2x2x4 slice. The times are simulated.
32 devices in a mesh: enc: 4 (over y, x), pool: 8 (over z, core).
Axes of the slice: x: 2, y: 2, z: 4, core: 2. Of those that a mesh axis runs over, the one named last changes fastest.
Arguments:
- encoded: bfloat16 [2048, 32, 128], P('pool', 'enc'), may hold values from -6 to 6
- slot_items: int32 [2048], replicated, may hold values from 0 to 2047, as said below
- lengths: int32 [2048], P(('enc', 'pool')), may hold values from 1 to 32
- token_mask: int32 [2048, 32], P(('enc', 'pool')), may hold values 0 or 1
Outputs:
- scores: float32 [2048, 192], P(('enc', 'pool'))
Inputs may be any that keep to these rules, and one draw needn't show every extreme that they name: `slot_items`: each item appears in exactly one slot. The slots d * 64 + p * 8 + j, for j below 8, hold items p * 256 to (p + 1) * 256 - 1, those whose encoder rows lie on pool index p.
All inputs are finite; a program needn't handle non-finite values. No bound on the sum of `token_mask` on one device may be relied on, other than what follows from the above.
Results may differ from a plain program's by a relative error of at most 0.00057.
Values may be sent and summed in bfloat16 or wider, within the bound.
No kernel may reach another device: no remote copies, remote signals or barrier semaphores. Data moves between devices by JAX's collectives and lax.ppermute only.
A program may use at most 64 MiB of HBM per device.

v0:
```python
import jax
import jax.numpy as jnp
from jax import lax
from jax.sharding import PartitionSpec as P


def tile_scores(query, query_bias, other, other_bias):
    tok, query_items, width = query.shape
    other_items = other.shape[1]
    rows = min(32, query_items)
    blocks = query_items // rows
    other_flat = other.reshape(tok * other_items, width)
    other_add = other_bias.astype(jnp.float32)[:, :, None]
    other_valid = other_bias == 0
    turned_all = jnp.transpose(query.reshape(tok, blocks, rows, width), (1, 0, 2, 3))
    adding_all = jnp.transpose(
        query_bias.astype(jnp.float32).reshape(tok, blocks, rows), (1, 0, 2)
    )[..., None]
    kept_all = jnp.transpose((query_bias == 0).reshape(tok, blocks, rows), (1, 0, 2))

    def one_block(operands):
        turned, adding, kept = operands
        flat = turned.reshape(tok * rows, width)
        dots_fore = jnp.einsum("ubh,qh->ubq", other, flat, preferred_element_type=jnp.float32)
        fore = jnp.max(dots_fore + other_add, axis=0).reshape(other_items, tok, rows)
        fore = jnp.sum(jnp.where(kept[None], fore, 0.0), axis=1)
        dots_back = jnp.einsum(
            "trh,ch->trc", turned, other_flat, preferred_element_type=jnp.float32
        )
        back = jnp.max(dots_back + adding, axis=0).reshape(rows, tok, other_items)
        back = jnp.sum(jnp.where(other_valid[None], back, 0.0), axis=1)
        return 0.5 * (fore.T + back)

    result = lax.map(one_block, (turned_all, adding_all, kept_all))
    return result.reshape(query_items, other_items)


def shards(encoded, slot_items, lengths, token_mask):
    n_enc = lax.axis_size("enc")
    n_pool = lax.axis_size("pool")
    owners = n_enc * n_pool
    group = encoded.shape[0]
    toks = encoded.shape[1]
    width = encoded.shape[2]
    items_dev = lengths.shape[0]
    per = items_dev // n_pool
    tok = n_enc * toks
    n_tok = items_dev * tok
    pool_index = lax.axis_index("pool")
    table = slot_items.reshape(owners, n_pool, per)
    mine = lax.dynamic_index_in_dim(table, pool_index, 1, keepdims=False) - pool_index * group
    outgoing = jnp.take(encoded, mine, axis=0, mode="clip")
    outgoing = jnp.transpose(outgoing, (2, 0, 1, 3))
    arrived = lax.all_to_all(outgoing, ("enc", "pool"), split_axis=1, concat_axis=1, tiled=True)
    slotted = arrived.reshape(tok, items_dev, width)
    values = slotted.astype(jnp.float32)
    normed = (values / jnp.sqrt(jnp.sum(values * values, axis=-1, keepdims=True) + 1e-06)).astype(
        jnp.bfloat16
    )
    position = jnp.arange(tok, dtype=jnp.int32)[None, :]
    valid = (position < lengths[:, None]) & ((position == 0) | (token_mask == 1))
    valid_tm = jnp.transpose(valid.reshape(items_dev, n_enc, toks), (2, 1, 0)).reshape(
        tok, items_dev
    )
    bias = jnp.where(valid_tm, 0.0, -4.0).astype(jnp.bfloat16)
    packed = jnp.concatenate([normed.reshape(n_tok, width), bias.reshape(-1, width)], axis=0)
    block = packed[:n_tok].reshape(tok, items_dev, width)
    parity = (pool_index ^ pool_index >> 1 ^ pool_index >> 2) & 1
    is_a = pool_index & 1 == 0

    def par(p):
        return (p ^ p >> 1 ^ p >> 2) & 1

    send_pairs = [(p, p ^ (4 if par(p) else 2)) for p in range(n_pool)]
    back_pairs = [(t, s) for s, t in send_pairs]
    chip_pairs = [(p, p ^ 1) for p in range(n_pool)]
    z_recv = lax.ppermute(packed, "pool", send_pairs)
    c_recv = lax.ppermute(packed, "pool", chip_pairs)

    def unpack(received):
        return (
            received[:n_tok].reshape(tok, items_dev, width),
            received[n_tok:].reshape(tok, items_dev),
        )

    half = items_dev // 2
    c_blk, c_bias = unpack(c_recv)
    query = jnp.where(is_a, block[:, :half], c_blk[:, half:])
    query_bias = jnp.where(is_a, bias[:, :half], c_bias[:, half:])
    other = jnp.where(is_a, c_blk, block)
    other_bias = jnp.where(is_a, c_bias, bias)
    part = tile_scores(query, query_bias, other, other_bias)
    part_recv = lax.ppermute(part, "pool", chip_pairs)
    joined = jnp.where(
        is_a, jnp.concatenate([part, part_recv], axis=0), jnp.concatenate([part_recv, part], axis=0)
    )
    tile0 = jnp.where(is_a, joined, joined.T)
    z_blk, z_bias = unpack(z_recv)
    tile_z = tile_scores(block, bias, z_blk, z_bias)
    tile_back = lax.ppermute(tile_z.T, "pool", back_pairs)
    other_items = tile_z.shape[1]
    ready = lax.optimization_barrier(jnp.concatenate([tile0, tile_z, tile_z], axis=1))
    column = jnp.arange(3 * other_items, dtype=jnp.int32)[None, :] // other_items
    back_here = column == 1 + parity
    return jnp.where(back_here, jnp.tile(tile_back, (1, 3)), ready)


def solution(mesh):
    in_specs = (P("pool", "enc", None), P(), P(("enc", "pool")), P(("enc", "pool"), None))
    out_specs = P(("enc", "pool"), None)
    return jax.shard_map(shards, mesh=mesh, in_specs=in_specs, out_specs=out_specs, check_vma=False)
```

profile of v0, /device:TPU:0, one launch (start us, length us, event | category | flops | bytes accessed | tf_op | source)
XLA Modules:
  0.0 54.5 jit_solution(16466838070889059354)
XLA Ops:
  0.0 0.8 %reshape.227 = s32[32,8,8]{2,1,0:T(8,128)S(1)} reshape(s32[2048]{0:T(1024)} %param.7) | data formatting | bytes 16384 | tf_op jit(solution)/shard_map/reshape | solution.py:50
  1.1 0.8 %gather_fusion = bf16[256,8,128]{2,1,0:T(8,128)(2,1)S(1)} fusion(bf16[256,8,128]{2,1,0:T(8,128)(2,1)S(1)} %copy-done, s32[1024]{0:T(1024)S(1)} %pad_clamp_fusion), kind=kCustom, calls=%fused_computation | custom fusion | bytes 1049600 | tf_op jit(solution)/shard_map/jit(_take)/gather | solution.py:52
  1.9 0.9 %copy.53 = bf16[8,32,8,128]{3,2,0,1:T(8,128)(2,1)} copy(bf16[8,32,8,128]{3,0,2,1:T(8,128)(2,1)S(1)} %bitcast.110) | data formatting | bytes 1048576 | tf_op jit(solution)/shard_map/transpose | solution.py:53
  2.8 7.3 %all-to-all-start = ((bf16[8,32,8,128]{3,2,0,1:T(8,128)(2,1)}), bf16[8,32,8,128]{3,2,0,1:T(8,128)(2,1)S(1)}, u32[]{:S(2)}, u32[]{:S(2)}) async-start(bf16[8,32,8,128]{3,2,0,1:T(8,128)(2,1)} %copy.53), calls=%async_computation | async-start | bytes 1048576 | tf_op jit(solution)/shard_map/all_to_all | solution.py:54
  10.4 16.0 %all-to-all-done = bf16[8,32,8,128]{3,2,0,1:T(8,128)(2,1)S(1)} async-done(((bf16[8,32,8,128]{3,2,0,1:T(8,128)(2,1)}), bf16[8,32,8,128]{3,2,0,1:T(8,128)(2,1)S(1)}, u32[]{:S(2)}, u32[]{:S(2)}) %all-to-all-start) | async-done | bytes 524320 | tf_op jit(solution)/shard_map/all_to_all | solution.py:54
  26.4 0.3 multiply_reduce_fusion
  27.0 0.3 fusion.3
  27.9 0.3 fusion.6
  28.3 1.3 %collective-permute-done.2 = bf16[2064,128]{1,0:T(8,128)(2,1)} collective-permute-done((bf16[2064,128]{1,0:T(8,128)(2,1)S(1)}, bf16[2064,128]{1,0:T(8,128)(2,1)}, u32[]{:S(2)}, u32[]{:S(2)}) %collective-permute-start.2) | collective-permute-done | bytes 528416 | tf_op jit(solution)/shard_map/ppermute | solution.py:78
  29.5 0.7 %slice.37 = bf16[16,128]{1,0:T(8,128)(2,1)S(1)} slice(bf16[2064,128]{1,0:T(8,128)(2,1)} %collective-permute-done.2), slice={[2048:2064], [0:128]} | slice | bytes 8192 | tf_op jit(solution)/shard_map/slice | solution.py:83
  30.5 1.4 %broadcast_select_fusion = (bf16[2048,128]{1,0:T(8,128)(2,1)S(1)}, bf16[2048,128]{1,0:T(8,128)(2,1)S(1)}) fusion(pred[]{:T(512)S(6)} %eq.71, bf16[2064,128]{1,0:T(8,128)(2,1)} %collective-permute-done.2, f32[2048]{0:T(1024)S(1)} %sqrt.21, f32[8,32,8,128]{3,2,1,0:T(8,128)S(1)} %copy_convert_fusion), kind=kLoop, calls=%fused_computation.27 | loop fusion | flops 786432 | bytes 2629633 | tf_op jit(solution)/shard_map/jit(_where)/select_n | solution.py:90
  31.9 0.2 fusion.7
  32.1 1.3 %add_reduce_fusion.2 = f32[32,2048]{1,0:T(8,128)S(1)} fusion(bf16[32,32,128]{2,1,0:T(8,128)(2,1)S(1)} %fusion.7, f32[32,32]{1,0:T(8,128)S(1)} %fusion.13, bf16[2048,128]{1,0:T(8,128)(2,1)S(1)} %get-tuple-element.143), kind=kOutput, calls=%fused_computation.13 | convolution fusion | flops 540999680 | bytes 1052672 | tf_op jit(solution)/shard_map/while/body/eval_jaxpr/trh,ch->trc/dot_general | solution.py:27
  33.4 1.3 %add_reduce_fusion.3 = f32[64,1024]{1,0:T(8,128)S(1)} fusion(f32[32,64]{1,0:T(8,128)S(1)} %fusion.11, bf16[32,64,128]{2,1,0:T(8,128)(2,1)S(1)} %bitcast.115, bf16[1024,128,1]{1,0,2:T(8,128)(2,1)S(1)} %bitcast.119), kind=kOutput, calls=%fused_computation.14 | convolution fusion | flops 540999680 | bytes 1056768 | tf_op jit(solution)/shard_map/while/body/eval_jaxpr/ubh,qh->ubq/dot_general | solution.py:24
  34.7 0.2 copy.59
  34.9 0.2 reshape.234
  35.2 0.2 select_reduce_fusion.3
  35.4 0.2 collective-permute-start.3
  35.6 7.2 %collective-permute-done = bf16[2064,128]{1,0:T(8,128)(2,1)S(1)} collective-permute-done((bf16[2064,128]{1,0:T(8,128)(2,1)S(1)}, bf16[2064,128]{1,0:T(8,128)(2,1)S(1)}, u32[]{:S(2)}, u32[]{:S(2)}) %collective-permute-start) | collective-permute-done | bytes 528416 | tf_op jit(solution)/shard_map/ppermute | solution.py:77
  43.0 6.7 %while.2 = (s32[]{:T(128)}, f32[2,32,64]{2,1,0:T(8,128)S(1)}, pred[2,32,32]{2,1,0:T(8,128)(4,1)S(1)}, bf16[2,32,32,128]{3,2,0,1:T(8,128)(2,1)S(1)}, bf16[32,64,1...) while((s32[]{:T(128)}, f32[2,32,64]{2,1,0:T(8,128)S(1)}, ...), condition=%wide.region_6.7_spmd, body=%wide.region_1.6_spmd.sunk | while | flops 1082261504 | bytes 4285557 | solution.py:34
  43.1 1.3 %add_reduce_fusion.6 = f32[32,2048]{1,0:T(8,128)S(1)} fusion(f32[32,32]{1,0:T(8,128)S(1)} %bitcast.116, bf16[2048,128]{1,0:T(8,128)(2,1)S(1)} %get-tuple-element.230, bf16[1,32,32,128]{3,2,0,1:T(8,128)(2,1)S(1)} %constant_dynamic-slice_fusion.5), kind=kOutput, calls=%fused_computation.1.clone.1 | convolution fusion | flops 540999680 | bytes 1052672 | tf_op jit(solution)/shard_map/while/body/eval_jaxpr/trh,ch->trc/dot_general | solution.py:27
  44.4 0.2 reshape.263
  44.7 1.3 %add_reduce_fusion.7 = f32[1024,64]{0,1:T(8,128)S(1)} fusion(f32[32,64]{1,0:T(8,128)S(1)} %bitcast.128, bf16[1024,128,1]{1,0,2:T(8,128)(2,1)S(1)} %bitcast.108, bf16[32,64,128]{2,1,0:T(8,128)(2,1)S(1)} %bitcast.113), kind=kOutput, calls=%fused_computation.2.clone.1 | convolution fusion | flops 540999680 | bytes 1056768 | tf_op jit(solution)/shard_map/while/body/eval_jaxpr/ubh,qh->ubq/dot_general | solution.py:24
  46.0 0.2 copy.72
  46.2 0.2 select_reduce_fusion.7
  46.5 1.3 %add_reduce_fusion.6 = f32[32,2048]{1,0:T(8,128)S(1)} fusion(f32[32,32]{1,0:T(8,128)S(1)} %bitcast.116, bf16[2048,128]{1,0:T(8,128)(2,1)S(1)} %get-tuple-element.230, bf16[1,32,32,128]{3,2,0,1:T(8,128)(2,1)S(1)} %constant_dynamic-slice_fusion.5), kind=kOutput, calls=%fused_computation.1.clone.1 | convolution fusion | flops 540999680 | bytes 1052672 | tf_op jit(solution)/shard_map/while/body/eval_jaxpr/trh,ch->trc/dot_general | solution.py:27
  47.7 0.2 reshape.263
  48.1 1.3 %add_reduce_fusion.7 = f32[1024,64]{0,1:T(8,128)S(1)} fusion(f32[32,64]{1,0:T(8,128)S(1)} %bitcast.128, bf16[1024,128,1]{1,0,2:T(8,128)(2,1)S(1)} %bitcast.108, bf16[32,64,128]{2,1,0:T(8,128)(2,1)S(1)} %bitcast.113), kind=kOutput, calls=%fused_computation.2.clone.1 | convolution fusion | flops 540999680 | bytes 1056768 | tf_op jit(solution)/shard_map/while/body/eval_jaxpr/ubh,qh->ubq/dot_general | solution.py:24
  49.3 0.2 copy.72
  49.5 0.2 select_reduce_fusion.7
  50.1 3.7 %collective-permute-done.1 = f32[64,64]{0,1:T(8,128)S(1)} collective-permute-done((f32[64,64]{0,1:T(8,128)S(1)}, f32[64,64]{0,1:T(8,128)S(1)}, u32[]{:S(2)}, u32[]{:S(2)}) %collective-permute-start.1) | collective-permute-done | bytes 16416 | tf_op jit(solution)/shard_map/ppermute | solution.py:100
  53.8 0.6 %broadcast_select_fusion.1 = f32[64,192]{1,0:T(8,128)} fusion(f32[64,192]{1,0:T(8,128)S(1)} %copy.61, f32[64,192]{1,0:T(8,128)S(1)} %pad_maximum_fusion.1, pred[192]{0:T(512)(128)(4,1)S(1)} %fusion.12), kind=kLoop, calls=%fused_computation.33 | loop fusion | flops 12288 | bytes 147648 | tf_op jit(solution)/shard_map/jit(_where)/select_n | solution.py:105
  (57 shorter events, 2.4 us)
Async XLA Ops:
  0.0 1.1 %copy-start = (bf16[256,8,128]{2,1,0:T(8,128)(2,1)S(1)}, bf16[256,8,128]{2,1,0:T(8,128)(2,1)}, u32[]{:S(2)}) copy-start(bf16[256,8,128]{2,1,0:T(8,128)(2,1)} %param.6) | copy-start | bytes 1572868
  1.9 8.2 %copy-start.1 = (s32[64,32]{0,1:T(8,128)S(1)}, s32[64,32]{0,1:T(8,128)}, u32[]{:S(2)}) copy-start(s32[64,32]{0,1:T(8,128)} %param.9) | copy-start | bytes 24580
  1.9 8.2 %copy-start.2 = (s32[64]{0:T(128)S(1)}, s32[64]{0:T(128)}, u32[]{:S(2)}) copy-start(s32[64]{0:T(128)} %param.8) | copy-start | bytes 772
  2.8 23.7 %all-to-all-start = ((bf16[8,32,8,128]{3,2,0,1:T(8,128)(2,1)}), bf16[8,32,8,128]{3,2,0,1:T(8,128)(2,1)S(1)}, u32[]{:S(2)}, u32[]{:S(2)}) async-start(bf16[8,32,8,128]{3,2,0,1:T(8,128)(2,1)} %copy.53), calls=%async_computation | async-start | bytes 1048576 | tf_op jit(solution)/shard_map/all_to_all | solution.py:54
  27.4 2.1 %collective-permute-start.2 = (bf16[2064,128]{1,0:T(8,128)(2,1)S(1)}, bf16[2064,128]{1,0:T(8,128)(2,1)}, u32[]{:S(2)}, u32[]{:S(2)}) collective-permute-start(bf16[2064,128]{1,0:T(8,128)(2,1)S(1)} %pad_maximum_fusion), channel_id=1, source_target_pairs={{0,1},{1,0},{2,3},{3,2},{4,5},{5,4},{6,7},{7,6},{8,9},{9,8},{10,11... | collective-permute-start | bytes 1585160 | tf_op jit(solution)/shard_map/ppermute | solution.py:78
  27.7 15.1 %collective-permute-start = (bf16[2064,128]{1,0:T(8,128)(2,1)S(1)}, bf16[2064,128]{1,0:T(8,128)(2,1)S(1)}, u32[]{:S(2)}, u32[]{:S(2)}) collective-permute-start(bf16[2064,128]{1,0:T(8,128)(2,1)S(1)} %pad_maximum_fusion), channel_id=1, source_target_pairs={{0,2},{1,5},{2,6},{3,1},{4,0},{5,7},{6,4},{7,3},{8,10},{9,13},{10,... | collective-permute-start | bytes 1585160 | tf_op jit(solution)/shard_map/ppermute | solution.py:77
  35.4 14.4 %collective-permute-start.3 = (f32[32,64]{1,0:T(8,128)S(1)}, f32[32,64]{1,0:T(8,128)S(1)}, u32[]{:S(2)}, u32[]{:S(2)}) collective-permute-start(f32[32,64]{1,0:T(8,128)S(1)} %fusion.8), channel_id=1, source_target_pairs={{0,1},{1,0},{2,3},{3,2},{4,5},{5,4},{6,7},{7,6},{8,9},{9,8},{10,11... | collective-permute-start | bytes 24584 | tf_op jit(solution)/shard_map/ppermute | solution.py:93
  49.8 4.0 %collective-permute-start.1 = (f32[64,64]{0,1:T(8,128)S(1)}, f32[64,64]{0,1:T(8,128)S(1)}, u32[]{:S(2)}, u32[]{:S(2)}) collective-permute-start(f32[64,64]{0,1:T(8,128)S(1)} %bitcast.126), channel_id=1, source_target_pairs={{2,0},{5,1},{6,2},{1,3},{0,4},{7,5},{4,6},{3,7},{10,8},{13,9},{14,... | collective-permute-start | bytes 49160 | tf_op jit(solution)/shard_map/ppermute | solution.py:100
where the time goes:
time: 54.8 us; the launch traced here: 54.5 us
  waiting for transfers between devices  28.2 us (51%)
  starting transfers between devices  7.69 us (14%)
  matrix products  7.58 us (14%)
  local copies, waits for them, and re-layouts  5.71 us (10%)
  other arithmetic  4.8 us (9%)
    all_to_all x1, waiting for transfers between devices, shards(): lax.all_to_all(outgoing, ('enc', 'pool'), split_axis=1, concat_axis=1, ti...  16 us
    all_to_all x1, starting transfers between devices, shards(): lax.all_to_all(outgoing, ('enc', 'pool'), split_axis=1, concat_axis=1, ti...  7.3 us
    ppermute x1, waiting for transfers between devices, shards(): z_recv = lax.ppermute(packed, 'pool', send_pairs)  7.19 us
    dot_general x3, matrix products, one_block(): jnp.einsum('ubh,qh->ubq', other, flat, preferred_element_type=jnp.float32)  3.79 us
    dot_general x3, matrix products, one_block(): jnp.einsum('trh,ch->trc', turned, other_flat, preferred_element_type=jnp....  3.79 us
    ppermute x1, waiting for transfers between devices, shards(): tile_back = lax.ppermute(tile_z.T, 'pool', back_pairs)  3.69 us
    select_n x1, other arithmetic, shards(): other = jnp.where(is_a, c_blk, block)  1.4 us
    ppermute x1, waiting for transfers between devices, shards(): c_recv = lax.ppermute(packed, 'pool', chip_pairs)  1.27 us
  transfers between devices with their start and end apart: 5, of which 4 were waited for; matrix products, arithmetic and copies ran while one was open for 25% of the time, Pallas kernels for 0%

commit v1 on v0

--- a/solution.py
+++ b/solution.py
@@ -2,6 +2,7 @@
 import jax.numpy as jnp
 from jax import lax
 from jax.sharding import PartitionSpec as P
+from jax.lax import all_to_all, axis_size
 
 
 def tile_scores(query, query_bias, other, other_bias):
@@ -51,7 +52,8 @@
     mine = lax.dynamic_index_in_dim(table, pool_index, 1, keepdims=False) - pool_index * group
     outgoing = jnp.take(encoded, mine, axis=0, mode="clip")
     outgoing = jnp.transpose(outgoing, (2, 0, 1, 3))
-    arrived = lax.all_to_all(outgoing, ("enc", "pool"), split_axis=1, concat_axis=1, tiled=True)
+    part_now = jnp.stack(jnp.split(outgoing, axis_size(("enc", "pool")), axis=1), axis=0)
+    arrived = jnp.concatenate(all_to_all(part_now, ("enc", "pool"), 0, 0), axis=1)
     slotted = arrived.reshape(tok, items_dev, width)
     values = slotted.astype(jnp.float32)
     normed = (values / jnp.sqrt(jnp.sum(values * values, axis=-1, keepdims=True) + 1e-06)).astype(

time: 54.8 us -> 73.6 us (1.34)
  local copies, waits for them, and re-layouts: 5.71 us -> 24.4 us
    unnamed x6 -> x37, local copies, waits for them, and re-layouts: 0.04 us -> 18.6 us
    transpose x1 -> x0, local copies, waits for them, and re-layouts: 0.89 us -> none  [shards(): outgoing = jnp.transpose(outgoing, (2, 0, 1, 3))]
  transfers between devices with their start and end apart: 5 -> 5, of which waited for: 4 -> 4; matrix products, arithmetic and copies ran while one was open for 25% -> 19% of each run, Pallas kernels for 0% -> 0%
where the time goes in v1:
time: 73.6 us; the launch traced here: 73.2 us
  waiting for transfers between devices  28.2 us (38%)
  local copies, waits for them, and re-layouts  24.4 us (33%)
  starting transfers between devices  7.7 us (10%)
  matrix products  7.6 us (10%)
  other arithmetic  4.85 us (7%)
    unnamed x37, local copies, waits for them, and re-layouts  18.6 us
    all_to_all x1, waiting for transfers between devices, shards(): all_to_all(part_now, ('enc', 'pool'), 0, 0)  16 us
    all_to_all x1, starting transfers between devices, shards(): all_to_all(part_now, ('enc', 'pool'), 0, 0)  7.3 us
    ppermute x1, waiting for transfers between devices, shards(): z_recv = lax.ppermute(packed, 'pool', send_pairs)  7.18 us
    dot_general x3, matrix products, one_block(): jnp.einsum('trh,ch->trc', turned, other_flat, preferred_element_type=jnp....  3.8 us
    dot_general x3, matrix products, one_block(): jnp.einsum('ubh,qh->ubq', other, flat, preferred_element_type=jnp.float32)  3.8 us
    ppermute x1, waiting for transfers between devices, shards(): tile_back = lax.ppermute(tile_z.T, 'pool', back_pairs)  3.69 us
  transfers between devices with their start and end apart: 5, of which 4 were waited for; matrix products, arithmetic and copies ran while one was open for 19% of the time, Pallas kernels for 0%

profile of v1, /device:TPU:0, one launch (start us, length us, event | category | flops | bytes accessed | tf_op | source)
XLA Modules:
  0.0 73.2 jit_solution(10220680917164848235)
XLA Ops:
  0.0 0.8 %reshape.229 = s32[32,8,8]{2,1,0:T(8,128)S(1)} reshape(s32[2048]{0:T(1024)} %param.7) | data formatting | bytes 16384 | tf_op jit(solution)/shard_map/reshape | solution.py:51
  1.1 0.8 %gather_fusion = bf16[256,8,128]{2,1,0:T(8,128)(2,1)S(1)} fusion(bf16[256,8,128]{2,1,0:T(8,128)(2,1)S(1)} %copy-done, s32[1024]{0:T(1024)S(1)} %pad_clamp_fusion), kind=kCustom, calls=%fused_computation | custom fusion | bytes 1049600 | tf_op jit(solution)/shard_map/jit(_take)/gather | solution.py:53
  2.5 0.6 constant_dynamic-update-slice_fusion.30
  3.1 0.6 constant_dynamic-update-slice_fusion.29
  3.7 0.6 constant_dynamic-update-slice_fusion.28
  6.1 0.6 constant_dynamic-update-slice_fusion.24
  8.5 0.6 constant_dynamic-update-slice_fusion.20
  9.1 0.6 constant_dynamic-update-slice_fusion.19
  10.3 0.6 constant_dynamic-update-slice_fusion.17
  12.7 0.6 constant_dynamic-update-slice_fusion.13
  13.3 0.6 constant_dynamic-update-slice_fusion.12
  13.9 0.6 constant_dynamic-update-slice_fusion.11
  15.1 0.6 constant_dynamic-update-slice_fusion.9
  16.3 0.6 constant_dynamic-update-slice_fusion.7
  17.5 0.6 constant_dynamic-update-slice_fusion.5
  18.7 0.6 constant_dynamic-update-slice_fusion.3
  20.5 0.6 constant_dynamic-update-slice_fusion
  21.1 7.3 %all-to-all-start = ((bf16[32,8,1,8,128]{4,1,3,2,0:T(8,128)(2,1)}), bf16[32,8,1,8,128]{4,1,3,2,0:T(8,128)(2,1)S(1)}, u32[]{:S(2)}, u32[]{:S(2)}) async-start(bf16[32,8,1,8,128]{4,1,3,2,0:T(8,128)(2,1)} %constant_dynamic-update-slice_fusion), calls=%async_computation | async-start | bytes 1048576 | tf_op jit(solution)/shard_map/all_to_all | solution.py:56
  28.7 16.0 %all-to-all-done = bf16[32,8,1,8,128]{4,1,3,2,0:T(8,128)(2,1)S(1)} async-done(((bf16[32,8,1,8,128]{4,1,3,2,0:T(8,128)(2,1)}), bf16[32,8,1,8,128]{4,1,3,2,0:T(8,128)(2,1)S(1)}, u32[]{:S(2)}, u32[]{:S(2)}) %all-to-all-start) | async-done | bytes 524320 | tf_op jit(solution)/shard_map/all_to_all | solution.py:56
  47.0 1.3 %collective-permute-done.2 = bf16[2064,128]{1,0:T(8,128)(2,1)} collective-permute-done((bf16[2064,128]{1,0:T(8,128)(2,1)S(1)}, bf16[2064,128]{1,0:T(8,128)(2,1)}, u32[]{:S(2)}, u32[]{:S(2)}) %collective-permute-start.2) | collective-permute-done | bytes 528416 | tf_op jit(solution)/shard_map/ppermute | solution.py:80
  48.3 0.7 slice.37
  49.2 1.4 %broadcast_select_fusion = (bf16[2048,128]{1,0:T(8,128)(2,1)S(1)}, bf16[2048,128]{1,0:T(8,128)(2,1)S(1)}) fusion(pred[]{:T(512)S(6)} %eq.71, bf16[2064,128]{1,0:T(8,128)(2,1)} %collective-permute-done.2, f32[2048]{0:T(1024)S(1)} %sqrt.21, f32[8,32,1,8,128]{4,3,1,0,2:T(8,128)S(1)} %copy.119), kind=kLoop, calls=%fused_computation.28 | loop fusion | flops 786432 | bytes 2629633 | tf_op jit(solution)/shard_map/jit(_where)/select_n | solution.py:92
  50.9 1.3 %add_reduce_fusion.2 = f32[32,2048]{1,0:T(8,128)S(1)} fusion(bf16[32,32,128]{2,1,0:T(8,128)(2,1)S(1)} %fusion.8, f32[32,32]{1,0:T(8,128)S(1)} %fusion.14, bf16[2048,128]{1,0:T(8,128)(2,1)S(1)} %get-tuple-element.143), kind=kOutput, calls=%fused_computation.13 | convolution fusion | flops 540999680 | bytes 1052672 | tf_op jit(solution)/shard_map/while/body/eval_jaxpr/trh,ch->trc/dot_general | solution.py:28
  52.1 1.3 %add_reduce_fusion.3 = f32[64,1024]{1,0:T(8,128)S(1)} fusion(f32[32,64]{1,0:T(8,128)S(1)} %fusion.12, bf16[32,64,128]{2,1,0:T(8,128)(2,1)S(1)} %bitcast.278, bf16[1024,128,1]{1,0,2:T(8,128)(2,1)S(1)} %bitcast.282), kind=kOutput, calls=%fused_computation.14 | convolution fusion | flops 540999680 | bytes 1056768 | tf_op jit(solution)/shard_map/while/body/eval_jaxpr/ubh,qh->ubq/dot_general | solution.py:25
  54.4 7.2 %collective-permute-done = bf16[2064,128]{1,0:T(8,128)(2,1)S(1)} collective-permute-done((bf16[2064,128]{1,0:T(8,128)(2,1)S(1)}, bf16[2064,128]{1,0:T(8,128)(2,1)S(1)}, u32[]{:S(2)}, u32[]{:S(2)}) %collective-permute-start) | collective-permute-done | bytes 528416 | tf_op jit(solution)/shard_map/ppermute | solution.py:79
  61.8 6.8 %while.2 = (s32[]{:T(128)}, f32[2,32,64]{2,1,0:T(8,128)S(1)}, pred[2,32,32]{2,1,0:T(8,128)(4,1)S(1)}, bf16[2,32,32,128]{3,2,0,1:T(8,128)(2,1)S(1)}, bf16[32,64,1...) while((s32[]{:T(128)}, f32[2,32,64]{2,1,0:T(8,128)S(1)}, ...), condition=%wide.region_6.7_spmd, body=%wide.region_1.6_spmd.sunk | while | flops 1082261504 | bytes 4285557 | solution.py:35
  61.8 1.3 %add_reduce_fusion.6 = f32[32,2048]{1,0:T(8,128)S(1)} fusion(f32[32,32]{1,0:T(8,128)S(1)} %bitcast.279, bf16[2048,128]{1,0:T(8,128)(2,1)S(1)} %get-tuple-element.230, bf16[1,32,32,128]{3,2,0,1:T(8,128)(2,1)S(1)} %constant_dynamic-slice_fusion.5), kind=kOutput, calls=%fused_computation.1.clone.1 | convolution fusion | flops 540999680 | bytes 1052672 | tf_op jit(solution)/shard_map/while/body/eval_jaxpr/trh,ch->trc/dot_general | solution.py:28
  63.4 1.3 %add_reduce_fusion.7 = f32[1024,64]{0,1:T(8,128)S(1)} fusion(f32[32,64]{1,0:T(8,128)S(1)} %bitcast.291, bf16[1024,128,1]{1,0,2:T(8,128)(2,1)S(1)} %bitcast.240, bf16[32,64,128]{2,1,0:T(8,128)(2,1)S(1)} %bitcast.276), kind=kOutput, calls=%fused_computation.2.clone.1 | convolution fusion | flops 540999680 | bytes 1056768 | tf_op jit(solution)/shard_map/while/body/eval_jaxpr/ubh,qh->ubq/dot_general | solution.py:25
  65.2 1.3 %add_reduce_fusion.6 = f32[32,2048]{1,0:T(8,128)S(1)} fusion(f32[32,32]{1,0:T(8,128)S(1)} %bitcast.279, bf16[2048,128]{1,0:T(8,128)(2,1)S(1)} %get-tuple-element.230, bf16[1,32,32,128]{3,2,0,1:T(8,128)(2,1)S(1)} %constant_dynamic-slice_fusion.5), kind=kOutput, calls=%fused_computation.1.clone.1 | convolution fusion | flops 540999680 | bytes 1052672 | tf_op jit(solution)/shard_map/while/body/eval_jaxpr/trh,ch->trc/dot_general | solution.py:28
  66.8 1.3 %add_reduce_fusion.7 = f32[1024,64]{0,1:T(8,128)S(1)} fusion(f32[32,64]{1,0:T(8,128)S(1)} %bitcast.291, bf16[1024,128,1]{1,0,2:T(8,128)(2,1)S(1)} %bitcast.240, bf16[32,64,128]{2,1,0:T(8,128)(2,1)S(1)} %bitcast.276), kind=kOutput, calls=%fused_computation.2.clone.1 | convolution fusion | flops 540999680 | bytes 1056768 | tf_op jit(solution)/shard_map/while/body/eval_jaxpr/ubh,qh->ubq/dot_general | solution.py:25
  68.8 3.7 %collective-permute-done.1 = f32[64,64]{0,1:T(8,128)S(1)} collective-permute-done((f32[64,64]{0,1:T(8,128)S(1)}, f32[64,64]{0,1:T(8,128)S(1)}, u32[]{:S(2)}, u32[]{:S(2)}) %collective-permute-start.1) | collective-permute-done | bytes 16416 | tf_op jit(solution)/shard_map/ppermute | solution.py:102
  72.6 0.6 broadcast_select_fusion.1
  (90 shorter events, 16.2 us)
Async XLA Ops:
  0.0 1.1 %copy-start = (bf16[256,8,128]{2,1,0:T(8,128)(2,1)S(1)}, bf16[256,8,128]{2,1,0:T(8,128)(2,1)}, u32[]{:S(2)}) copy-start(bf16[256,8,128]{2,1,0:T(8,128)(2,1)} %param.6) | copy-start | bytes 1572868
  1.9 26.6 %copy-start.1 = (s32[64,32]{0,1:T(8,128)S(1)}, s32[64,32]{0,1:T(8,128)}, u32[]{:S(2)}) copy-start(s32[64,32]{0,1:T(8,128)} %param.9) | copy-start | bytes 24580
  1.9 26.6 %copy-start.2 = (s32[64]{0:T(128)S(1)}, s32[64]{0:T(128)}, u32[]{:S(2)}) copy-start(s32[64]{0:T(128)} %param.8) | copy-start | bytes 772
  21.1 23.7 %all-to-all-start = ((bf16[32,8,1,8,128]{4,1,3,2,0:T(8,128)(2,1)}), bf16[32,8,1,8,128]{4,1,3,2,0:T(8,128)(2,1)S(1)}, u32[]{:S(2)}, u32[]{:S(2)}) async-start(bf16[32,8,1,8,128]{4,1,3,2,0:T(8,128)(2,1)} %constant_dynamic-update-slice_fusion), calls=%async_computation | async-start | bytes 1048576 | tf_op jit(solution)/shard_map/all_to_all | solution.py:56
  46.2 2.1 %collective-permute-start.2 = (bf16[2064,128]{1,0:T(8,128)(2,1)S(1)}, bf16[2064,128]{1,0:T(8,128)(2,1)}, u32[]{:S(2)}, u32[]{:S(2)}) collective-permute-start(bf16[2064,128]{1,0:T(8,128)(2,1)S(1)} %pad_maximum_fusion), channel_id=1, source_target_pairs={{0,1},{1,0},{2,3},{3,2},{4,5},{5,4},{6,7},{7,6},{8,9},{9,8},{10,11... | collective-permute-start | bytes 1585160 | tf_op jit(solution)/shard_map/ppermute | solution.py:80
  46.5 15.1 %collective-permute-start = (bf16[2064,128]{1,0:T(8,128)(2,1)S(1)}, bf16[2064,128]{1,0:T(8,128)(2,1)S(1)}, u32[]{:S(2)}, u32[]{:S(2)}) collective-permute-start(bf16[2064,128]{1,0:T(8,128)(2,1)S(1)} %pad_maximum_fusion), channel_id=1, source_target_pairs={{0,2},{1,5},{2,6},{3,1},{4,0},{5,7},{6,4},{7,3},{8,10},{9,13},{10,... | collective-permute-start | bytes 1585160 | tf_op jit(solution)/shard_map/ppermute | solution.py:79
  54.2 14.4 %collective-permute-start.3 = (f32[32,64]{1,0:T(8,128)S(1)}, f32[32,64]{1,0:T(8,128)S(1)}, u32[]{:S(2)}, u32[]{:S(2)}) collective-permute-start(f32[32,64]{1,0:T(8,128)S(1)} %fusion.9), channel_id=1, source_target_pairs={{0,1},{1,0},{2,3},{3,2},{4,5},{5,4},{6,7},{7,6},{8,9},{9,8},{10,11... | collective-permute-start | bytes 24584 | tf_op jit(solution)/shard_map/ppermute | solution.py:95
  68.5 4.0 %collective-permute-start.1 = (f32[64,64]{0,1:T(8,128)S(1)}, f32[64,64]{0,1:T(8,128)S(1)}, u32[]{:S(2)}, u32[]{:S(2)}) collective-permute-start(f32[64,64]{0,1:T(8,128)S(1)} %bitcast.289), channel_id=1, source_target_pairs={{2,0},{5,1},{6,2},{1,3},{0,4},{7,5},{4,6},{3,7},{10,8},{13,9},{14,... | collective-permute-start | bytes 49160 | tf_op jit(solution)/shard_map/ppermute | solution.py:102
